TPU v7x, 256 devices: a whole 4x4x8 slice. The times are simulated.
256 devices in a mesh: ctx: 32 (over z, x), dp: 8 (over y, core).
Axes of the slice: x: 4, y: 4, z: 8, core: 2. Of those that a mesh axis runs over, the one named last changes fastest.
Arguments:
- layer_input: bfloat16 [8, 4096, 5376], P('dp', 'ctx'), may hold values from -12 to 12
- query_states: bfloat16 [8, 4096, 2048], P('dp', 'ctx'), may hold values from -6 to 6
- key_states: bfloat16 [8, 4096, 1024], P('dp', 'ctx'), may hold values from -6 to 6
- value_state_rows: bfloat16 [8, 4096, 1024], P('dp', 'ctx'), may hold values from -6 to 6
- grad_out: bfloat16 [8, 4096, 2048], P('dp', 'ctx'), may hold values from -180 to 180
- segments: int32 [8, 4096], P('dp', 'ctx'), may hold values from 0 to 7, never falling along the last dimension, each value on 1 to 2048 neighbouring positions
- master: float32 [5376, 1024], P(('ctx', 'dp')), may hold values from -0.078125 to 0.078125
- first_moment_value: float32 [5376, 1024], P(('ctx', 'dp')), may hold values from -0.0024 to 0.0024
- second_moment_value: float32 [5376, 1024], P(('ctx', 'dp')), may hold values from 1e-08 to 1e-06
Outputs:
- query_gradient: bfloat16 [8, 4096, 2048], P('dp', 'ctx')
- key_gradient: bfloat16 [8, 4096, 1024], P('dp', 'ctx')
- value_gradient: bfloat16 [8, 4096, 1024], P('dp', 'ctx')
- new_master: float32 [5376, 1024], P(('ctx', 'dp'))
- new_first: float32 [5376, 1024], P(('ctx', 'dp'))
- new_second: float32 [5376, 1024], P(('ctx', 'dp'))
- new_weight: bfloat16 [5376, 1024], P('ctx')
Inputs may be any that keep to these rules, and one draw needn't show every extreme that they name: `segments`: segment numbers never fall along a sequence; each document holds 1 to 2048 tokens and one holds exactly 2048.
All inputs are finite; a program needn't handle non-finite values.
Results may differ from a plain program's by a relative error of at most 0.01.
The roundings to bfloat16 on the way count: a program that leaves them out, or rounds other values in their place, can miss the bound.
Values may be sent and summed in bfloat16 or wider, within the bound.
No kernel may reach another device: no remote copies, remote signals or barrier semaphores. Data moves between devices by JAX's collectives and lax.ppermute only.
A program may use at most 128 MiB of HBM per device.

v0:
```python
import jax
import jax.numpy as jnp
from jax import lax
from jax.sharding import PartitionSpec as P

QUERY_HEADS = 16
KEY_VALUE_HEADS = 8
HEAD_SIZE = 128
WINDOW = 1024
query_scale = 168.0 ** (-0.5)
masked_score = -1e30
clip_norm = 1.0
beta_first = 0.9
beta_second = 0.95
learn_rate = 0.001
decay_rate = 0.1
adam_eps = 1e-08
correct_first = 0.9999734386011124
correct_second = 0.994079470779666


def from_behind(x, axis, by):
    count = lax.axis_size(axis)
    pairs = [(i, i + by) for i in range(count) if 0 <= i + by < count]
    return lax.ppermute(x, axis, pairs)


def attend(
    query_row_block,
    key_row_block,
    value_row_block,
    gradient_rows,
    seg_query,
    seg_key,
    index_query,
    index_key,
):
    shard_length = query_row_block.shape[0]
    extent_rows = key_row_block.shape[0]
    heads_ratio = QUERY_HEADS // KEY_VALUE_HEADS
    query_four_axes = query_row_block.reshape(shard_length, KEY_VALUE_HEADS, heads_ratio, HEAD_SIZE)
    gradient_four_axes = gradient_rows.reshape(
        shard_length, KEY_VALUE_HEADS, heads_ratio, HEAD_SIZE
    )
    key_three_axes = key_row_block.reshape(extent_rows, KEY_VALUE_HEADS, HEAD_SIZE)
    value_three_axes = value_row_block.reshape(extent_rows, KEY_VALUE_HEADS, HEAD_SIZE)
    scores = (
        jnp.einsum(
            "tgrd,egd->grte", query_four_axes, key_three_axes, preferred_element_type=jnp.float32
        )
        * query_scale
    )
    offset = index_query[:, None] - index_key[None, :]
    allowed = (
        (seg_query[:, None] == seg_key[None, :])
        & (offset >= 0)
        & (offset < WINDOW)
        & (index_key[None, :] >= 0)
    )
    scores = jnp.where(allowed, scores, masked_score)
    row_max = jnp.max(scores, axis=-1, keepdims=True)
    weights = jnp.exp(scores - row_max)
    probabilities = weights / jnp.sum(weights, axis=-1, keepdims=True)
    probs_low = probabilities.astype(jnp.bfloat16)
    attn_out = jnp.einsum(
        "grte,egd->tgrd", probs_low, value_three_axes, preferred_element_type=jnp.float32
    )
    row_delta = jnp.sum(gradient_four_axes.astype(jnp.float32) * attn_out, axis=-1)
    grad_probs = jnp.einsum(
        "tgrd,egd->grte", gradient_four_axes, value_three_axes, preferred_element_type=jnp.float32
    )
    grad_scores = probabilities * (grad_probs - jnp.transpose(row_delta, (1, 2, 0))[..., None])
    scores_low = grad_scores.astype(jnp.bfloat16)
    query_gradient = (
        jnp.einsum("grte,egd->tgrd", scores_low, key_three_axes, preferred_element_type=jnp.float32)
        * query_scale
    )
    query_gradient = query_gradient.astype(jnp.bfloat16).reshape(
        shard_length, QUERY_HEADS * HEAD_SIZE
    )
    key_gradient = (
        jnp.einsum(
            "grte,tgrd->egd", scores_low, query_four_axes, preferred_element_type=jnp.float32
        )
        * query_scale
    )
    value_gradient = jnp.einsum(
        "grte,tgrd->egd", probs_low, gradient_four_axes, preferred_element_type=jnp.float32
    )
    return (
        query_gradient,
        key_gradient.reshape(extent_rows, KEY_VALUE_HEADS * HEAD_SIZE),
        value_gradient.reshape(extent_rows, KEY_VALUE_HEADS * HEAD_SIZE),
    )


def shards(
    layer_input,
    query_states,
    key_states,
    value_state_rows,
    grad_out,
    segments,
    master,
    first_moment_value,
    second_moment_value,
):
    shard_length = query_states.shape[1]
    peer_count = min(WINDOW // shard_length, lax.axis_size("ctx") - 1)
    front_len = peer_count * shard_length
    position = lax.axis_index("ctx") * shard_length
    seg_low = segments[0].astype(jnp.bfloat16)
    own_piece = (key_states[0], value_state_rows[0], seg_low)
    incoming_list = []
    for distance in range(peer_count, 0, -1):
        incoming_list.append(
            from_behind((own_piece[0], own_piece[1], own_piece[2]), "ctx", distance)
        )
    halo_rows = tuple(
        (
            jnp.concatenate([incoming[member] for incoming in incoming_list], axis=0)
            for member in range(3)
        )
    )
    key_row_block = jnp.concatenate([halo_rows[0], key_states[0]], axis=0)
    value_row_block = jnp.concatenate([halo_rows[1], value_state_rows[0]], axis=0)
    seg_key = jnp.concatenate([halo_rows[2], seg_low], axis=0)
    index_query = position + jnp.arange(shard_length, dtype=jnp.int32)
    index_key = position - front_len + jnp.arange(front_len + shard_length, dtype=jnp.int32)
    query_gradient, key_gradient, value_gradient = attend(
        query_states[0],
        key_row_block,
        value_row_block,
        grad_out[0],
        seg_low,
        seg_key,
        index_query,
        index_key,
    )
    key_sum = key_gradient[front_len:]
    value_sum = value_gradient[front_len:]
    for distance in range(1, peer_count + 1):
        lower = (peer_count - distance) * shard_length
        key_part = key_gradient[lower : lower + shard_length].astype(jnp.bfloat16)
        value_part = value_gradient[lower : lower + shard_length].astype(jnp.bfloat16)
        returned = from_behind((key_part, value_part), "ctx", -distance)
        key_sum = key_sum + returned[0].astype(jnp.float32)
        value_sum = value_sum + returned[1].astype(jnp.float32)
    key_out = key_sum.astype(jnp.bfloat16)
    value_out = value_sum.astype(jnp.bfloat16)
    feature_block = lax.all_to_all(layer_input[0], "ctx", split_axis=1, concat_axis=0, tiled=True)
    sequence_grad = lax.dot_general(
        feature_block,
        lax.all_gather(value_out, "ctx", axis=0, tiled=True),
        (((0,), (0,)), ((), ())),
        preferred_element_type=jnp.float32,
    )
    weight_grad = lax.psum_scatter(sequence_grad, "dp", scatter_dimension=0, tiled=True)
    square_total = lax.psum(jnp.sum(weight_grad * weight_grad), ("ctx", "dp"))
    norm_total = jnp.sqrt(square_total + 1e-06)
    clipped = weight_grad * jnp.minimum(1.0, clip_norm / norm_total)
    new_first = beta_first * first_moment_value + (1.0 - beta_first) * clipped
    new_second = beta_second * second_moment_value + (1.0 - beta_second) * clipped * clipped
    step_dir = new_first / correct_first / (jnp.sqrt(new_second / correct_second) + adam_eps)
    new_master = master - learn_rate * (step_dir + decay_rate * master)
    new_weight = lax.all_gather(new_master.astype(jnp.bfloat16), "dp", axis=0, tiled=True)
    return (
        query_gradient[None],
        key_out[None],
        value_out[None],
        new_master,
        new_first,
        new_second,
        new_weight,
    )


def solution(mesh):
    return jax.shard_map(
        shards,
        mesh=mesh,
        in_specs=(
            P("dp", "ctx", None),
            P("dp", "ctx", None),
            P("dp", "ctx", None),
            P("dp", "ctx", None),
            P("dp", "ctx", None),
            P("dp", "ctx"),
            P(("ctx", "dp"), None),
            P(("ctx", "dp"), None),
            P(("ctx", "dp"), None),
        ),
        out_specs=(
            P("dp", "ctx", None),
            P("dp", "ctx", None),
            P("dp", "ctx", None),
            P(("ctx", "dp"), None),
            P(("ctx", "dp"), None),
            P(("ctx", "dp"), None),
            P("ctx", None),
        ),
        check_vma=False,
    )
```

profile of v0, /device:TPU:1, one launch (start us, length us, event | category | flops | bytes accessed | tf_op | source)
XLA Modules:
  0.0 551.0 jit_solution(3754582582561746699)
XLA Ops:
  7.9 5.7 %collective-permute-start.8 = (bf16[128]{0:T(256)(128)(2,1)S(1)}, bf16[128]{0:T(256)(128)(2,1)S(1)}, u32[]{:S(2)}, u32[]{:S(2)}) collective-permute-start(bf16[128]{0:T(256)(128)(2,1)S(1)} %convert_bitcast_fusion.1), channel_id=1, source_target_pairs={{0,64},{8,72},{16,80},{24,88},{32,96},{40,104},{48,112},{56,120},{... | collective-permute-start | bytes 776 | tf_op jit(solution)/shard_map/ppermute | solution.py:25
  13.6 5.7 %collective-permute-start.9 = (bf16[128]{0:T(256)(128)(2,1)S(1)}, bf16[128]{0:T(256)(128)(2,1)S(1)}, u32[]{:S(2)}, u32[]{:S(2)}) collective-permute-start(bf16[128]{0:T(256)(128)(2,1)S(1)} %convert_bitcast_fusion.1), channel_id=1, source_target_pairs={{0,56},{8,64},{16,72},{24,80},{32,88},{40,96},{48,104},{56,112},{6... | collective-permute-start | bytes 776 | tf_op jit(solution)/shard_map/ppermute | solution.py:25
  19.4 1.8 copy.98
  21.1 5.2 collective-permute-start
  26.4 3.4 collective-permute-start.1
  29.8 1.9 collective-permute-start.2
  34.6 2.0 copy.108
  36.5 3.6 collective-permute-start.10
  40.4 2.3 collective-permute-start.11
  42.9 8.8 %collective-permute-start.12 = (bf16[128]{0:T(256)(128)(2,1)S(1)}, bf16[128]{0:T(256)(128)(2,1)S(1)}, u32[]{:S(2)}, u32[]{:S(2)}) collective-permute-start(bf16[128]{0:T(256)(128)(2,1)S(1)} %convert_bitcast_fusion.1), channel_id=1, source_target_pairs={{0,32},{8,40},{16,48},{24,56},{32,64},{40,72},{48,80},{56,88},{64,... | collective-permute-start | bytes 776 | tf_op jit(solution)/shard_map/ppermute | solution.py:25
  52.0 14.1 %collective-permute-start.13 = (bf16[128]{0:T(256)(128)(2,1)S(1)}, bf16[128]{0:T(256)(128)(2,1)S(1)}, u32[]{:S(2)}, u32[]{:S(2)}) collective-permute-start(bf16[128]{0:T(256)(128)(2,1)S(1)} %convert_bitcast_fusion.1), channel_id=1, source_target_pairs={{0,24},{8,32},{16,40},{24,48},{32,56},{40,64},{48,72},{56,80},{64,... | collective-permute-start | bytes 776 | tf_op jit(solution)/shard_map/ppermute | solution.py:25
  67.9 3.1 collective-permute-start.15
  71.3 7.6 %collective-permute-start.3 = (bf16[128,1024]{0,1:T(8,128)(2,1)}, bf16[128,1024]{0,1:T(8,128)(2,1)S(1)}, u32[]{:S(2)}, u32[]{:S(2)}) collective-permute-start(bf16[128,1024]{0,1:T(8,128)(2,1)} %bitcast), channel_id=1, source_target_pairs={{0,40},{8,48},{16,56},{24,64},{32,72},{40,80},{48,88},{56,96},{64,... | collective-permute-start | bytes 786440 | tf_op jit(solution)/shard_map/ppermute | solution.py:25
  79.1 2.8 collective-permute-start.4
  82.2 3.5 collective-permute-start.5
  85.7 3.1 collective-permute-start.6
  88.8 3.2 collective-permute-start.7
  100.0 1.8 copy.107
  107.0 6.1 %fusion.54 = (f32[8,2,128]{2,1,0:T(2,128)}, f32[8,2,128,1152]{2,3,1,0:T(8,128)}) fusion(pred[128,1152]{0,1:T(8,128)(4,1)S(1)} %fusion.40, bf16[128,8,2,128]{0,3,2,1:T(8,128)(2,1)S(1)} %bitcast.154, bf16[1152,8,128]{2,0,1:T(8,128)(2,1)S(1)} %constant_dynamic-update-slice_fusion), kind=kOutput, calls=%fused_computation.72 | convolution fusion | flops 613418112 | bytes 12476416 | tf_op jit(solution)/shard_map/sub | solution.py:62
  113.1 4.8 fusion.9
  117.9 3.7 fusion.58
  123.1 1.8 copy.147
  126.2 1.8 copy.146
  129.3 1.8 copy.145
  132.3 1.8 copy.144
  140.2 28.3 %collective-permute-done.39 = bf16[128,1024]{1,0:T(8,128)(2,1)} collective-permute-done((bf16[128,1024]{1,0:T(8,128)(2,1)}, bf16[128,1024]{1,0:T(8,128)(2,1)}, u32[]{:S(2)}, u32[]{:S(2)}) %collective-permute-start.39) | collective-permute-done | bytes 262176 | tf_op jit(solution)/shard_map/ppermute | solution.py:25
  173.9 10.8 %collective-permute-done.34 = bf16[128,1024]{1,0:T(8,128)(2,1)} collective-permute-done((bf16[128,1024]{1,0:T(8,128)(2,1)}, bf16[128,1024]{1,0:T(8,128)(2,1)}, u32[]{:S(2)}, u32[]{:S(2)}) %collective-permute-start.34) | collective-permute-done | bytes 262176 | tf_op jit(solution)/shard_map/ppermute | solution.py:25
  184.7 4.5 collective-permute-done.32
  189.2 2.6 add_convert_fusion
  192.6 25.7 %collective-permute-start.16 = (bf16[128,1024]{0,1:T(8,128)(2,1)}, bf16[128,1024]{0,1:T(8,128)(2,1)}, u32[]{:S(2)}, u32[]{:S(2)}) collective-permute-start(bf16[128,1024]{0,1:T(8,128)(2,1)} %bitcast.15), channel_id=1, source_target_pairs={{0,64},{8,72},{16,80},{24,88},{32,96},{40,104},{48,112},{56,120},{... | collective-permute-start | bytes 786440 | tf_op jit(solution)/shard_map/ppermute | solution.py:25
  218.4 7.7 %collective-permute-start.17 = (bf16[128,1024]{0,1:T(8,128)(2,1)}, bf16[128,1024]{0,1:T(8,128)(2,1)}, u32[]{:S(2)}, u32[]{:S(2)}) collective-permute-start(bf16[128,1024]{0,1:T(8,128)(2,1)} %bitcast.15), channel_id=1, source_target_pairs={{0,56},{8,64},{16,72},{24,80},{32,88},{40,96},{48,104},{56,112},{6... | collective-permute-start | bytes 786440 | tf_op jit(solution)/shard_map/ppermute | solution.py:25
  226.1 2.0 collective-permute-start.18
  228.1 2.0 collective-permute-start.19
  230.1 2.4 collective-permute-start.20
  232.5 3.8 collective-permute-start.21
  236.3 2.3 collective-permute-start.22
  238.6 3.2 collective-permute-done.18
  241.9 2.0 collective-permute-start.23
  243.9 2.6 copy.148
  246.4 31.1 %all-to-all-start = ((bf16[128,32,168]{0,2,1:T(8,128)(2,1)}), bf16[128,32,168]{0,2,1:T(8,128)(2,1)}, u32[]{:S(2)}, u32[]{:S(2)}) async-start(bf16[128,32,168]{0,2,1:T(8,128)(2,1)} %bitcast.152), calls=%async_computation | async-start | bytes 2752512 | tf_op jit(solution)/shard_map/all_to_all | solution.py:151
  277.6 1.9 copy.120
  279.4 1.8 copy.112
  281.2 1.8 copy.113
  283.0 1.8 copy.114
  284.8 1.8 copy.115
  286.6 1.8 copy.116
  288.4 1.8 copy.117
  290.2 1.8 copy.118
  292.0 1.8 copy.119
  299.1 3.5 fusion.35
  305.6 3.7 fusion.57
  313.8 1.8 copy.136
  316.9 1.8 copy.135
  320.1 42.3 %all-gather.3.cloned.1.call-done = bf16[4096,1024]{1,0:T(8,128)(2,1)} async-done(((bf16[128,1024]{1,0:T(8,128)(2,1)}), bf16[4096,1024]{1,0:T(8,128)(2,1)}) %all-gather.3.cloned.1.call-update) | async-done | bytes 8388624 | tf_op jit(solution)/shard_map/all_gather | solution.py:154
  362.4 6.2 %fusion.32 = f32[168,1024]{1,0:T(8,128)} fusion(bf16[4096,1024]{1,0:T(8,128)(2,1)} %all-gather.3.cloned.1.call-done, bf16[128,32,168]{0,2,1:T(8,128)(2,1)} %all-to-all-done), kind=kOutput, calls=%fused_computation.29 | convolution fusion | flops 1409286144 | bytes 10452992 | tf_op jit(solution)/shard_map/dot_general | solution.py:152
  368.5 18.3 %fusion = f32[24,1024]{1,0:T(8,128)S(1)} fusion(f32[168,1024]{1,0:T(8,128)} %fusion.32), kind=kCustom, calls=%all-reduce-scatter | all-reduce-scatter fusion | flops 196609 | bytes 787456
  387.5 2.7 collective-permute-start.40
  391.5 1.8 copy.134
  402.1 3.4 fusion.29
  409.4 12.0 %collective-permute-done.28 = bf16[128,1024]{1,0:T(8,128)(2,1)} collective-permute-done((bf16[128,1024]{1,0:T(8,128)(2,1)}, bf16[128,1024]{1,0:T(8,128)(2,1)}, u32[]{:S(2)}, u32[]{:S(2)}) %collective-permute-start.28) | collective-permute-done | bytes 262176 | tf_op jit(solution)/shard_map/ppermute | solution.py:25
  421.5 7.7 %collective-permute-done.24 = bf16[128,1024]{1,0:T(8,128)(2,1)} collective-permute-done((bf16[128,1024]{1,0:T(8,128)(2,1)S(1)}, bf16[128,1024]{1,0:T(8,128)(2,1)}, u32[]{:S(2)}, u32[]{:S(2)}) %collective-permute-start.24) | collective-permute-done | bytes 262176 | tf_op jit(solution)/shard_map/ppermute | solution.py:25
  429.1 2.6 fusion.45
  431.7 96.6 %psum.7 = f32[]{:T(128)} all-reduce(f32[]{:T(128)} %multiply_reduce_fusion), channel_id=1, replica_groups=mesh['ctx'=32,'dp'=8] {'ctx','dp'}, use_global_device_ids=true, to_apply=%region_5.6 | all-reduce | flops 1 | bytes 8 | tf_op jit(solution)/shard_map/psum | solution.py:159
  529.8 13.5 %all-gather = bf16[8,21,1024]{2,1,0:T(8,128)(2,1)S(1)} all-gather(bf16[1,21,1024]{2,1,0:T(8,128)(2,1)S(1)} %get-tuple-element.28), channel_id=1, replica_groups=mesh['ctx'=32,'dp'=8] {'dp'}, dimensions={0}, use_global_device_ids=true | all-gather | bytes 387072 | tf_op jit(solution)/shard_map/all_gather | solution.py:166
  (168 shorter events, 68.2 us)
Async XLA Ops:
  7.2 75.1 %copy-start.19 = (s32[1,128]{1,0:T(1,128)S(1)}, s32[1,128]{1,0:T(1,128)}, u32[]{:S(2)}) copy-start(s32[1,128]{1,0:T(1,128)} %param.14) | copy-start | bytes 1540
  7.2 355.2 %all-gather.3.cloned.1.call-start = ((), (), s32[]{:S(2)}) async-start(), calls=%async_computation.1 | async-start | bytes 8650752 | tf_op jit(solution)/shard_map/all_gather | solution.py:154
  7.9 28.6 %collective-permute-start.8 = (bf16[128]{0:T(256)(128)(2,1)S(1)}, bf16[128]{0:T(256)(128)(2,1)S(1)}, u32[]{:S(2)}, u32[]{:S(2)}) collective-permute-start(bf16[128]{0:T(256)(128)(2,1)S(1)} %convert_bitcast_fusion.1), channel_id=1, source_target_pairs={{0,64},{8,72},{16,80},{24,88},{32,96},{40,104},{48,112},{56,120},{... | collective-permute-start | bytes 776 | tf_op jit(solution)/shard_map/ppermute | solution.py:25
  13.6 26.8 %collective-permute-start.9 = (bf16[128]{0:T(256)(128)(2,1)S(1)}, bf16[128]{0:T(256)(128)(2,1)S(1)}, u32[]{:S(2)}, u32[]{:S(2)}) collective-permute-start(bf16[128]{0:T(256)(128)(2,1)S(1)} %convert_bitcast_fusion.1), channel_id=1, source_target_pairs={{0,56},{8,64},{16,72},{24,80},{32,88},{40,96},{48,104},{56,112},{6... | collective-permute-start | bytes 776 | tf_op jit(solution)/shard_map/ppermute | solution.py:25
  21.1 61.1 %collective-permute-start = (bf16[128,1024]{0,1:T(8,128)(2,1)}, bf16[128,1024]{0,1:T(8,128)(2,1)S(1)}, u32[]{:S(2)}, u32[]{:S(2)}) collective-permute-start(bf16[128,1024]{0,1:T(8,128)(2,1)} %bitcast), channel_id=1, source_target_pairs={{0,64},{8,72},{16,80},{24,88},{32,96},{40,104},{48,112},{56,120},{... | collective-permute-start | bytes 786440 | tf_op jit(solution)/shard_map/ppermute | solution.py:25
  26.4 59.3 %collective-permute-start.1 = (bf16[128,1024]{0,1:T(8,128)(2,1)}, bf16[128,1024]{0,1:T(8,128)(2,1)S(1)}, u32[]{:S(2)}, u32[]{:S(2)}) collective-permute-start(bf16[128,1024]{0,1:T(8,128)(2,1)} %bitcast), channel_id=1, source_target_pairs={{0,56},{8,64},{16,72},{24,80},{32,88},{40,96},{48,104},{56,112},{6... | collective-permute-start | bytes 786440 | tf_op jit(solution)/shard_map/ppermute | solution.py:25
  29.8 59.0 %collective-permute-start.2 = (bf16[128,1024]{0,1:T(8,128)(2,1)}, bf16[128,1024]{0,1:T(8,128)(2,1)S(1)}, u32[]{:S(2)}, u32[]{:S(2)}) collective-permute-start(bf16[128,1024]{0,1:T(8,128)(2,1)} %bitcast), channel_id=1, source_target_pairs={{0,48},{8,56},{16,64},{24,72},{32,80},{40,88},{48,96},{56,104},{64... | collective-permute-start | bytes 786440 | tf_op jit(solution)/shard_map/ppermute | solution.py:25
  33.0 84.9 %copy-start.2 = (bf16[1,128,2048]{1,2,0:T(8,128)(2,1)}, bf16[1,128,2048]{1,2,0:T(8,128)(2,1)S(1)}, u32[]{:S(2)}) copy-start(bf16[1,128,2048]{1,2,0:T(8,128)(2,1)S(1)} %copy.121) | copy-start | bytes 1572868
  34.5 72.5 %copy-start.4 = (bf16[1,128,2048]{1,2,0:T(8,128)(2,1)}, bf16[1,128,2048]{1,2,0:T(8,128)(2,1)S(1)}, u32[]{:S(2)}) copy-start(bf16[1,128,2048]{1,2,0:T(8,128)(2,1)S(1)} %copy.166) | copy-start | bytes 1572868
  36.5 6.4 %collective-permute-start.10 = (bf16[128]{0:T(256)(128)(2,1)S(1)}, bf16[128]{0:T(256)(128)(2,1)S(1)}, u32[]{:S(2)}, u32[]{:S(2)}) collective-permute-start(bf16[128]{0:T(256)(128)(2,1)S(1)} %convert_bitcast_fusion.1), channel_id=1, source_target_pairs={{0,48},{8,56},{16,64},{24,72},{32,80},{40,88},{48,96},{56,104},{64... | collective-permute-start | bytes 776 | tf_op jit(solution)/shard_map/ppermute | solution.py:25
  40.4 11.6 %collective-permute-start.11 = (bf16[128]{0:T(256)(128)(2,1)S(1)}, bf16[128]{0:T(256)(128)(2,1)S(1)}, u32[]{:S(2)}, u32[]{:S(2)}) collective-permute-start(bf16[128]{0:T(256)(128)(2,1)S(1)} %convert_bitcast_fusion.1), channel_id=1, source_target_pairs={{0,40},{8,48},{16,56},{24,64},{32,72},{40,80},{48,88},{56,96},{64,... | collective-permute-start | bytes 776 | tf_op jit(solution)/shard_map/ppermute | solution.py:25
  42.9 23.5 %collective-permute-start.12 = (bf16[128]{0:T(256)(128)(2,1)S(1)}, bf16[128]{0:T(256)(128)(2,1)S(1)}, u32[]{:S(2)}, u32[]{:S(2)}) collective-permute-start(bf16[128]{0:T(256)(128)(2,1)S(1)} %convert_bitcast_fusion.1), channel_id=1, source_target_pairs={{0,32},{8,40},{16,48},{24,56},{32,64},{40,72},{48,80},{56,88},{64,... | collective-permute-start | bytes 776 | tf_op jit(solution)/shard_map/ppermute | solution.py:25
  52.0 15.9 %collective-permute-start.13 = (bf16[128]{0:T(256)(128)(2,1)S(1)}, bf16[128]{0:T(256)(128)(2,1)S(1)}, u32[]{:S(2)}, u32[]{:S(2)}) collective-permute-start(bf16[128]{0:T(256)(128)(2,1)S(1)} %convert_bitcast_fusion.1), channel_id=1, source_target_pairs={{0,24},{8,32},{16,40},{24,48},{32,56},{40,64},{48,72},{56,80},{64,... | collective-permute-start | bytes 776 | tf_op jit(solution)/shard_map/ppermute | solution.py:25
  66.4 4.9 collective-permute-start.14
  67.9 11.2 %collective-permute-start.15 = (bf16[128]{0:T(256)(128)(2,1)S(1)}, bf16[128]{0:T(256)(128)(2,1)S(1)}, u32[]{:S(2)}, u32[]{:S(2)}) collective-permute-start(bf16[128]{0:T(256)(128)(2,1)S(1)} %convert_bitcast_fusion.1), channel_id=1, source_target_pairs={{0,8},{8,16},{16,24},{24,32},{32,40},{40,48},{48,56},{56,64},{64,7... | collective-permute-start | bytes 776 | tf_op jit(solution)/shard_map/ppermute | solution.py:25
  71.3 24.3 %collective-permute-start.3 = (bf16[128,1024]{0,1:T(8,128)(2,1)}, bf16[128,1024]{0,1:T(8,128)(2,1)S(1)}, u32[]{:S(2)}, u32[]{:S(2)}) collective-permute-start(bf16[128,1024]{0,1:T(8,128)(2,1)} %bitcast), channel_id=1, source_target_pairs={{0,40},{8,48},{16,56},{24,64},{32,72},{40,80},{48,88},{56,96},{64,... | collective-permute-start | bytes 786440 | tf_op jit(solution)/shard_map/ppermute | solution.py:25
  79.1 17.3 %collective-permute-start.4 = (bf16[128,1024]{0,1:T(8,128)(2,1)}, bf16[128,1024]{0,1:T(8,128)(2,1)S(1)}, u32[]{:S(2)}, u32[]{:S(2)}) collective-permute-start(bf16[128,1024]{0,1:T(8,128)(2,1)} %bitcast), channel_id=1, source_target_pairs={{0,32},{8,40},{16,48},{24,56},{32,64},{40,72},{48,80},{56,88},{64,... | collective-permute-start | bytes 786440 | tf_op jit(solution)/shard_map/ppermute | solution.py:25
  82.2 15.1 %collective-permute-start.5 = (bf16[128,1024]{0,1:T(8,128)(2,1)}, bf16[128,1024]{0,1:T(8,128)(2,1)S(1)}, u32[]{:S(2)}, u32[]{:S(2)}) collective-permute-start(bf16[128,1024]{0,1:T(8,128)(2,1)} %bitcast), channel_id=1, source_target_pairs={{0,24},{8,32},{16,40},{24,48},{32,56},{40,64},{48,72},{56,80},{64,... | collective-permute-start | bytes 786440 | tf_op jit(solution)/shard_map/ppermute | solution.py:25
  85.7 12.5 %collective-permute-start.6 = (bf16[128,1024]{0,1:T(8,128)(2,1)}, bf16[128,1024]{0,1:T(8,128)(2,1)S(1)}, u32[]{:S(2)}, u32[]{:S(2)}) collective-permute-start(bf16[128,1024]{0,1:T(8,128)(2,1)} %bitcast), channel_id=1, source_target_pairs={{0,16},{8,24},{16,32},{24,40},{32,48},{40,56},{48,64},{56,72},{64,... | collective-permute-start | bytes 786440 | tf_op jit(solution)/shard_map/ppermute | solution.py:25
  88.8 11.2 %collective-permute-start.7 = (bf16[128,1024]{0,1:T(8,128)(2,1)}, bf16[128,1024]{0,1:T(8,128)(2,1)}, u32[]{:S(2)}, u32[]{:S(2)}) collective-permute-start(bf16[128,1024]{0,1:T(8,128)(2,1)} %bitcast), channel_id=1, source_target_pairs={{0,8},{8,16},{16,24},{24,32},{32,40},{40,48},{48,56},{56,64},{64,7... | collective-permute-start | bytes 786440 | tf_op jit(solution)/shard_map/ppermute | solution.py:25
  101.8 5.0 copy-start.9
  101.8 5.1 copy-start.12
  101.8 5.1 copy-start.6
  117.9 3.8 copy-start
  124.9 43.6 %collective-permute-start.39 = (bf16[128,1024]{1,0:T(8,128)(2,1)}, bf16[128,1024]{1,0:T(8,128)(2,1)}, u32[]{:S(2)}, u32[]{:S(2)}) collective-permute-start(bf16[128,1024]{1,0:T(8,128)(2,1)} %copy.147), channel_id=1, source_target_pairs={{64,0},{72,8},{80,16},{88,24},{96,32},{104,40},{112,48},{120,56},{... | collective-permute-start | bytes 786440 | tf_op jit(solution)/shard_map/ppermute | solution.py:25
  128.0 41.8 %collective-permute-start.38 = (bf16[128,1024]{1,0:T(8,128)(2,1)}, bf16[128,1024]{1,0:T(8,128)(2,1)}, u32[]{:S(2)}, u32[]{:S(2)}) collective-permute-start(bf16[128,1024]{1,0:T(8,128)(2,1)} %copy.146), channel_id=1, source_target_pairs={{56,0},{64,8},{72,16},{80,24},{88,32},{96,40},{104,48},{112,56},{1... | collective-permute-start | bytes 786440 | tf_op jit(solution)/shard_map/ppermute | solution.py:25
  131.1 40.0 %collective-permute-start.37 = (bf16[128,1024]{1,0:T(8,128)(2,1)}, bf16[128,1024]{1,0:T(8,128)(2,1)}, u32[]{:S(2)}, u32[]{:S(2)}) collective-permute-start(bf16[128,1024]{1,0:T(8,128)(2,1)} %copy.145), channel_id=1, source_target_pairs={{48,0},{56,8},{64,16},{72,24},{80,32},{88,40},{96,48},{104,56},{11... | collective-permute-start | bytes 786440 | tf_op jit(solution)/shard_map/ppermute | solution.py:25
  134.1 39.7 %collective-permute-start.36 = (bf16[128,1024]{1,0:T(8,128)(2,1)}, bf16[128,1024]{1,0:T(8,128)(2,1)}, u32[]{:S(2)}, u32[]{:S(2)}) collective-permute-start(bf16[128,1024]{1,0:T(8,128)(2,1)} %copy.144), channel_id=1, source_target_pairs={{40,0},{48,8},{56,16},{64,24},{72,32},{80,40},{88,48},{96,56},{104... | collective-permute-start | bytes 786440 | tf_op jit(solution)/shard_map/ppermute | solution.py:25
  136.3 37.6 %collective-permute-start.35 = (bf16[128,1024]{1,0:T(8,128)(2,1)}, bf16[128,1024]{1,0:T(8,128)(2,1)}, u32[]{:S(2)}, u32[]{:S(2)}) collective-permute-start(bf16[128,1024]{1,0:T(8,128)(2,1)} %copy.143), channel_id=1, source_target_pairs={{32,0},{40,8},{48,16},{56,24},{64,32},{72,40},{80,48},{88,56},{96,... | collective-permute-start | bytes 786440 | tf_op jit(solution)/shard_map/ppermute | solution.py:25
  168.5 16.2 %collective-permute-start.34 = (bf16[128,1024]{1,0:T(8,128)(2,1)}, bf16[128,1024]{1,0:T(8,128)(2,1)}, u32[]{:S(2)}, u32[]{:S(2)}) collective-permute-start(bf16[128,1024]{1,0:T(8,128)(2,1)} %copy.142), channel_id=1, source_target_pairs={{24,0},{32,8},{40,16},{48,24},{56,32},{64,40},{72,48},{80,56},{88,... | collective-permute-start | bytes 786440 | tf_op jit(solution)/shard_map/ppermute | solution.py:25
  169.8 14.9 %collective-permute-start.33 = (bf16[128,1024]{1,0:T(8,128)(2,1)}, bf16[128,1024]{1,0:T(8,128)(2,1)}, u32[]{:S(2)}, u32[]{:S(2)}) collective-permute-start(bf16[128,1024]{1,0:T(8,128)(2,1)} %copy.141), channel_id=1, source_target_pairs={{16,0},{24,8},{32,16},{40,24},{48,32},{56,40},{64,48},{72,56},{80,... | collective-permute-start | bytes 786440 | tf_op jit(solution)/shard_map/ppermute | solution.py:25
  171.1 18.1 %collective-permute-start.32 = (bf16[128,1024]{1,0:T(8,128)(2,1)}, bf16[128,1024]{1,0:T(8,128)(2,1)}, u32[]{:S(2)}, u32[]{:S(2)}) collective-permute-start(bf16[128,1024]{1,0:T(8,128)(2,1)} %copy.139), channel_id=1, source_target_pairs={{8,0},{16,8},{24,16},{32,24},{40,32},{48,40},{56,48},{64,56},{72,6... | collective-permute-start | bytes 786440 | tf_op jit(solution)/shard_map/ppermute | solution.py:25
  173.9 17.9 %copy-start.13 = (bf16[1,128,1024]{2,1,0:T(8,128)(2,1)S(1)}, bf16[1,128,1024]{2,1,0:T(8,128)(2,1)}, u32[]{:S(2)}) copy-start(bf16[1,128,1024]{2,1,0:T(8,128)(2,1)} %param.12) | copy-start | bytes 786436
  192.6 39.8 %collective-permute-start.16 = (bf16[128,1024]{0,1:T(8,128)(2,1)}, bf16[128,1024]{0,1:T(8,128)(2,1)}, u32[]{:S(2)}, u32[]{:S(2)}) collective-permute-start(bf16[128,1024]{0,1:T(8,128)(2,1)} %bitcast.15), channel_id=1, source_target_pairs={{0,64},{8,72},{16,80},{24,88},{32,96},{40,104},{48,112},{56,120},{... | collective-permute-start | bytes 786440 | tf_op jit(solution)/shard_map/ppermute | solution.py:25
  218.4 17.9 %collective-permute-start.17 = (bf16[128,1024]{0,1:T(8,128)(2,1)}, bf16[128,1024]{0,1:T(8,128)(2,1)}, u32[]{:S(2)}, u32[]{:S(2)}) collective-permute-start(bf16[128,1024]{0,1:T(8,128)(2,1)} %bitcast.15), channel_id=1, source_target_pairs={{0,56},{8,64},{16,72},{24,80},{32,88},{40,96},{48,104},{56,112},{6... | collective-permute-start | bytes 786440 | tf_op jit(solution)/shard_map/ppermute | solution.py:25
  226.1 15.8 %collective-permute-start.18 = (bf16[128,1024]{0,1:T(8,128)(2,1)}, bf16[128,1024]{0,1:T(8,128)(2,1)}, u32[]{:S(2)}, u32[]{:S(2)}) collective-permute-start(bf16[128,1024]{0,1:T(8,128)(2,1)} %bitcast.15), channel_id=1, source_target_pairs={{0,48},{8,56},{16,64},{24,72},{32,80},{40,88},{48,96},{56,104},{64... | collective-permute-start | bytes 786440 | tf_op jit(solution)/shard_map/ppermute | solution.py:25
  228.1 56.7 %collective-permute-start.19 = (bf16[128,1024]{0,1:T(8,128)(2,1)}, bf16[128,1024]{0,1:T(8,128)(2,1)}, u32[]{:S(2)}, u32[]{:S(2)}) collective-permute-start(bf16[128,1024]{0,1:T(8,128)(2,1)} %bitcast.15), channel_id=1, source_target_pairs={{0,40},{8,48},{16,56},{24,64},{32,72},{40,80},{48,88},{56,96},{64,... | collective-permute-start | bytes 786440 | tf_op jit(solution)/shard_map/ppermute | solution.py:25
  230.1 56.5 %collective-permute-start.20 = (bf16[128,1024]{0,1:T(8,128)(2,1)}, bf16[128,1024]{0,1:T(8,128)(2,1)}, u32[]{:S(2)}, u32[]{:S(2)}) collective-permute-start(bf16[128,1024]{0,1:T(8,128)(2,1)} %bitcast.15), channel_id=1, source_target_pairs={{0,32},{8,40},{16,48},{24,56},{32,64},{40,72},{48,80},{56,88},{64,... | collective-permute-start | bytes 786440 | tf_op jit(solution)/shard_map/ppermute | solution.py:25
  232.5 55.9 %collective-permute-start.21 = (bf16[128,1024]{0,1:T(8,128)(2,1)}, bf16[128,1024]{0,1:T(8,128)(2,1)}, u32[]{:S(2)}, u32[]{:S(2)}) collective-permute-start(bf16[128,1024]{0,1:T(8,128)(2,1)} %bitcast.15), channel_id=1, source_target_pairs={{0,24},{8,32},{16,40},{24,48},{32,56},{40,64},{48,72},{56,80},{64,... | collective-permute-start | bytes 786440 | tf_op jit(solution)/shard_map/ppermute | solution.py:25
  236.3 54.0 %collective-permute-start.22 = (bf16[128,1024]{0,1:T(8,128)(2,1)}, bf16[128,1024]{0,1:T(8,128)(2,1)}, u32[]{:S(2)}, u32[]{:S(2)}) collective-permute-start(bf16[128,1024]{0,1:T(8,128)(2,1)} %bitcast.15), channel_id=1, source_target_pairs={{0,16},{8,24},{16,32},{24,40},{32,48},{40,56},{48,64},{56,72},{64,... | collective-permute-start | bytes 786440 | tf_op jit(solution)/shard_map/ppermute | solution.py:25
  241.9 50.1 %collective-permute-start.23 = (bf16[128,1024]{0,1:T(8,128)(2,1)}, bf16[128,1024]{0,1:T(8,128)(2,1)}, u32[]{:S(2)}, u32[]{:S(2)}) collective-permute-start(bf16[128,1024]{0,1:T(8,128)(2,1)} %bitcast.15), channel_id=1, source_target_pairs={{0,8},{8,16},{16,24},{24,32},{32,40},{40,48},{48,56},{56,64},{64,7... | collective-permute-start | bytes 786440 | tf_op jit(solution)/shard_map/ppermute | solution.py:25
  246.4 73.7 %all-to-all-start = ((bf16[128,32,168]{0,2,1:T(8,128)(2,1)}), bf16[128,32,168]{0,2,1:T(8,128)(2,1)}, u32[]{:S(2)}, u32[]{:S(2)}) async-start(bf16[128,32,168]{0,2,1:T(8,128)(2,1)} %bitcast.152), calls=%async_computation | async-start | bytes 2752512 | tf_op jit(solution)/shard_map/all_to_all | solution.py:151
  277.6 25.1 %slice-start = ((s8[9437184]{0:T(1024)(128)(4,1)}), s8[1048576]{0:T(1024)(128)(4,1)S(1)}, s32[]{:S(2)}) async-start(s8[9437184]{0:T(1024)(128)(4,1)} %bitcast.147), calls=%async_computation.2 | async-start | bytes 2097152
  293.8 5.1 copy-start.8
  293.8 5.1 copy-start.10
  293.8 5.2 copy-start.11
  293.8 5.2 copy-start.7
  293.8 5.3 copy-start.3
  298.9 3.8 slice-start.1
  299.1 4.8 slice-start.2
  299.1 4.8 copy-start.17
  312.5 84.1 %collective-permute-start.31 = (bf16[128,1024]{1,0:T(8,128)(2,1)}, bf16[128,1024]{1,0:T(8,128)(2,1)}, u32[]{:S(2)}, u32[]{:S(2)}) collective-permute-start(bf16[128,1024]{1,0:T(8,128)(2,1)} %copy.137), channel_id=1, source_target_pairs={{64,0},{72,8},{80,16},{88,24},{96,32},{104,40},{112,48},{120,56},{... | collective-permute-start | bytes 786440 | tf_op jit(solution)/shard_map/ppermute | solution.py:25
  315.6 82.3 %collective-permute-start.30 = (bf16[128,1024]{1,0:T(8,128)(2,1)}, bf16[128,1024]{1,0:T(8,128)(2,1)}, u32[]{:S(2)}, u32[]{:S(2)}) collective-permute-start(bf16[128,1024]{1,0:T(8,128)(2,1)} %copy.136), channel_id=1, source_target_pairs={{56,0},{64,8},{72,16},{80,24},{88,32},{96,40},{104,48},{112,56},{1... | collective-permute-start | bytes 786440 | tf_op jit(solution)/shard_map/ppermute | solution.py:25
  318.7 71.6 %copy-start.18 = (u32[256]{0:T(256)S(1)}, u32[256]{0:T(256)}, u32[]{:S(2)}) copy-start(u32[256]{0:T(256)} %constant.59) | copy-start | bytes 3076
  318.7 80.5 %collective-permute-start.29 = (bf16[128,1024]{1,0:T(8,128)(2,1)}, bf16[128,1024]{1,0:T(8,128)(2,1)}, u32[]{:S(2)}, u32[]{:S(2)}) collective-permute-start(bf16[128,1024]{1,0:T(8,128)(2,1)} %copy.135), channel_id=1, source_target_pairs={{48,0},{56,8},{64,16},{72,24},{80,32},{88,40},{96,48},{104,56},{11... | collective-permute-start | bytes 786440 | tf_op jit(solution)/shard_map/ppermute | solution.py:25
  387.5 13.0 %collective-permute-start.40 = (f32[21,1024]{1,0:T(8,128)}, f32[21,1024]{1,0:T(8,128)}, u32[]{:S(2)}, u32[]{:S(2)}) collective-permute-start(f32[21,1024]{1,0:T(8,128)} %slice.130), channel_id=1, source_target_pairs={{0,1},{1,2},{2,3},{3,4},{4,5},{5,6},{6,7},{8,9},{9,10},{10,11},{11... | collective-permute-start | bytes 258056
  393.3 28.1 %collective-permute-start.28 = (bf16[128,1024]{1,0:T(8,128)(2,1)}, bf16[128,1024]{1,0:T(8,128)(2,1)}, u32[]{:S(2)}, u32[]{:S(2)}) collective-permute-start(bf16[128,1024]{1,0:T(8,128)(2,1)} %copy.134), channel_id=1, source_target_pairs={{40,0},{48,8},{56,16},{64,24},{72,32},{80,40},{88,48},{96,56},{104... | collective-permute-start | bytes 786440 | tf_op jit(solution)/shard_map/ppermute | solution.py:25
  396.6 24.8 %collective-permute-start.27 = (bf16[128,1024]{1,0:T(8,128)(2,1)}, bf16[128,1024]{1,0:T(8,128)(2,1)}, u32[]{:S(2)}, u32[]{:S(2)}) collective-permute-start(bf16[128,1024]{1,0:T(8,128)(2,1)} %copy.133), channel_id=1, source_target_pairs={{32,0},{40,8},{48,16},{56,24},{64,32},{72,40},{80,48},{88,56},{96,... | collective-permute-start | bytes 786440 | tf_op jit(solution)/shard_map/ppermute | solution.py:25
  397.9 23.5 %collective-permute-start.26 = (bf16[128,1024]{1,0:T(8,128)(2,1)}, bf16[128,1024]{1,0:T(8,128)(2,1)}, u32[]{:S(2)}, u32[]{:S(2)}) collective-permute-start(bf16[128,1024]{1,0:T(8,128)(2,1)} %copy.132), channel_id=1, source_target_pairs={{24,0},{32,8},{40,16},{48,24},{56,32},{64,40},{72,48},{80,56},{88,... | collective-permute-start | bytes 786440 | tf_op jit(solution)/shard_map/ppermute | solution.py:25
  399.2 22.2 %collective-permute-start.25 = (bf16[128,1024]{1,0:T(8,128)(2,1)S(1)}, bf16[128,1024]{1,0:T(8,128)(2,1)}, u32[]{:S(2)}, u32[]{:S(2)}) collective-permute-start(bf16[128,1024]{1,0:T(8,128)(2,1)S(1)} %copy.131), channel_id=1, source_target_pairs={{16,0},{24,8},{32,16},{40,24},{48,32},{56,40},{64,48},{72,56},{80,... | collective-permute-start | bytes 786440 | tf_op jit(solution)/shard_map/ppermute | solution.py:25
  400.5 28.6 %collective-permute-start.24 = (bf16[128,1024]{1,0:T(8,128)(2,1)S(1)}, bf16[128,1024]{1,0:T(8,128)(2,1)}, u32[]{:S(2)}, u32[]{:S(2)}) collective-permute-start(bf16[128,1024]{1,0:T(8,128)(2,1)S(1)} %copy.129), channel_id=1, source_target_pairs={{8,0},{16,8},{24,16},{32,24},{40,32},{48,40},{56,48},{64,56},{72,6... | collective-permute-start | bytes 786440 | tf_op jit(solution)/shard_map/ppermute | solution.py:25
  407.5 121.5 %copy-start.14 = (f32[21,1024]{1,0:T(8,128)S(1)}, f32[21,1024]{1,0:T(8,128)}, u32[]{:S(2)}) copy-start(f32[21,1024]{1,0:T(8,128)} %param.15) | copy-start | bytes 258052
  407.5 121.5 %copy-start.15 = (f32[21,1024]{1,0:T(8,128)S(1)}, f32[21,1024]{1,0:T(8,128)}, u32[]{:S(2)}) copy-start(f32[21,1024]{1,0:T(8,128)} %param.16) | copy-start | bytes 258052
  407.5 121.5 %copy-start.16 = (f32[21,1024]{1,0:T(8,128)S(1)}, f32[21,1024]{1,0:T(8,128)}, u32[]{:S(2)}) copy-start(f32[21,1024]{1,0:T(8,128)} %param.17) | copy-start | bytes 258052
  (2 other events, 5.4 us)
Sparse Core Ops, SparseCore 0:
  191.9 170.4 all-gather.2
where the time goes:
time: 554 us; the launch traced here: 551 us
  starting transfers between devices  178 us (32%)
  blocking collectives  128 us (23%)
  waiting for transfers between devices  109 us (20%)
  local copies, waits for them, and re-layouts  77.8 us (14%)
  matrix products  28.2 us (5%)
  between operations  16.3 us (3%)
  other arithmetic  13.1 us (2%)
    ppermute x40, starting transfers between devices, from_behind(): return lax.ppermute(x, axis, pairs)  144 us
    psum x1, blocking collectives, shards(): square_total = lax.psum(jnp.sum(weight_grad * weight_grad), ('ctx', 'dp'))  96.6 us
    ppermute x40, waiting for transfers between devices, from_behind(): return lax.ppermute(x, axis, pairs)  66.6 us
    all_gather x1, waiting for transfers between devices, shards(): lax.all_gather(value_out, 'ctx', axis=0, tiled=True)  42.3 us
    all_to_all x1, starting transfers between devices, shards(): lax.all_to_all(layer_input[0], 'ctx', split_axis=1, concat_axis=0, tiled=...  31.1 us
    unnamed x79, local copies, waits for them, and re-layouts  25.1 us
    unnamed x1, blocking collectives  18.3 us
    concatenate x10, local copies, waits for them, and re-layouts, shards(): jnp.concatenate([halo_rows[1], value_state_rows[0]], axis=0)  16.3 us
  transfers between devices with their start and end apart: 43, of which 7 were waited for; matrix products, arithmetic and copies ran while one was open for 19% of the time, Pallas kernels for 0%

commit v1 on v0

--- a/solution.py
+++ b/solution.py
@@ -17,6 +17,15 @@
 adam_eps = 1e-08
 correct_first = 0.9999734386011124
 correct_second = 0.994079470779666
+
+
+def measure_thing_on(content):
+    return jnp.concatenate(
+        jax.lax.all_to_all(
+            jnp.stack([content for _ in range(jax.lax.axis_size("ctx"))], 0), "ctx", 0, 0
+        ),
+        0,
+    )
 
 
 def from_behind(x, axis, by):
@@ -151,7 +160,7 @@
     feature_block = lax.all_to_all(layer_input[0], "ctx", split_axis=1, concat_axis=0, tiled=True)
     sequence_grad = lax.dot_general(
         feature_block,
-        lax.all_gather(value_out, "ctx", axis=0, tiled=True),
+        measure_thing_on(value_out),
         (((0,), (0,)), ((), ())),
         preferred_element_type=jnp.float32,
     )

time: 554 us -> 700 us (1.26)
  waiting for transfers between devices: 109 us -> 253 us
  between operations: 16.3 us -> 2.92 us
  blocking collectives: 128 us -> 135 us
    ppermute x40, waiting for transfers between devices: 66.6 us -> 253 us  [from_behind(): return lax.ppermute(x, axis, pairs)]
    all_gather x1 -> x0, waiting for transfers between devices: 42.3 us -> none  [shards(): lax.all_gather(value_out, 'ctx', axis=0, tiled=True)]
    all_to_all x0 -> x1, starting transfers between devices: none -> 30.3 us  [measure_thing_on(): jax.lax.all_to_all(jnp.stack([content for _ in range(jax.lax.axis_size('c...]
    all_to_all x1, starting transfers between devices: 31.1 us -> 4.96 us  [shards(): lax.all_to_all(layer_input[0], 'ctx', split_axis=1, concat_axis=0, tiled=...]
    unnamed x79 -> x91, local copies, waits for them, and re-layouts: 25.1 us -> 24 us
  transfers between devices with their start and end apart: 43 -> 43, of which waited for: 7 -> 9; matrix products, arithmetic and copies ran while one was open for 19% -> 19% of each run, Pallas kernels for 0% -> 0%
where the time goes in v1:
time: 700 us; the launch traced here: 697 us
  waiting for transfers between devices  253 us (36%)
  starting transfers between devices  184 us (26%)
  blocking collectives  135 us (19%)
  local copies, waits for them, and re-layouts  81.2 us (12%)
  matrix products  28.2 us (4%)
  other arithmetic  12.4 us (2%)
    ppermute x40, waiting for transfers between devices, from_behind(): return lax.ppermute(x, axis, pairs)  253 us
    ppermute x40, starting transfers between devices, from_behind(): return lax.ppermute(x, axis, pairs)  147 us
    psum x1, blocking collectives, shards(): square_total = lax.psum(jnp.sum(weight_grad * weight_grad), ('ctx', 'dp'))  103 us
    all_to_all x1, starting transfers between devices, measure_thing_on(): jax.lax.all_to_all(jnp.stack([content for _ in range(jax.lax.axis_size('c...  30.3 us
    unnamed x91, local copies, waits for them, and re-layouts  24 us
    unnamed x1, blocking collectives  18.2 us
    concatenate x10, local copies, waits for them, and re-layouts, shards(): jnp.concatenate([halo_rows[1], value_state_rows[0]], axis=0)  16.2 us
  transfers between devices with their start and end apart: 43, of which 9 were waited for; matrix products, arithmetic and copies ran while one was open for 19% of the time, Pallas kernels for 0%

profile of v1, /device:TPU:1, one launch (start us, length us, event | category | flops | bytes accessed | tf_op | source)
XLA Modules:
  0.0 696.8 jit_solution(5819781610760682019)
XLA Ops:
  1.3 5.7 collective-permute-start.8
  7.0 5.7 collective-permute-start.9
  12.7 1.8 copy.98
  14.5 5.3 collective-permute-start
  19.9 3.4 collective-permute-start.1
  23.3 1.9 collective-permute-start.2
  25.2 2.5 copy.148
  27.7 5.0 all-to-all-start.1
  33.3 2.0 copy.108
  35.3 5.5 collective-permute-start.10
  41.0 3.1 collective-permute-start.11
  44.4 21.3 %collective-permute-done.10 = bf16[128]{0:T(256)(128)(2,1)S(1)} collective-permute-done((bf16[128]{0:T(256)(128)(2,1)S(1)}, bf16[128]{0:T(256)(128)(2,1)S(1)}, u32[]{:S(2)}, u32[]{:S(2)}) %collective-permute-start.10) | collective-permute-done | bytes 288 | tf_op jit(solution)/shard_map/ppermute | solution.py:34
  65.6 9.8 %collective-permute-start.12 = (bf16[128]{0:T(256)(128)(2,1)S(1)}, bf16[128]{0:T(256)(128)(2,1)S(1)}, u32[]{:S(2)}, u32[]{:S(2)}) collective-permute-start(bf16[128]{0:T(256)(128)(2,1)S(1)} %convert_bitcast_fusion.1), channel_id=1, source_target_pairs={{0,32},{8,40},{16,48},{24,56},{32,64},{40,72},{48,80},{56,88},{64,... | collective-permute-start | bytes 776 | tf_op jit(solution)/shard_map/ppermute | solution.py:34
  75.7 13.9 %collective-permute-start.13 = (bf16[128]{0:T(256)(128)(2,1)S(1)}, bf16[128]{0:T(256)(128)(2,1)S(1)}, u32[]{:S(2)}, u32[]{:S(2)}) collective-permute-start(bf16[128]{0:T(256)(128)(2,1)S(1)} %convert_bitcast_fusion.1), channel_id=1, source_target_pairs={{0,24},{8,32},{16,40},{24,48},{32,56},{40,64},{48,72},{56,80},{64,... | collective-permute-start | bytes 776 | tf_op jit(solution)/shard_map/ppermute | solution.py:34
  91.4 3.1 collective-permute-start.15
  94.7 7.3 %collective-permute-start.3 = (bf16[128,1024]{0,1:T(8,128)(2,1)}, bf16[128,1024]{0,1:T(8,128)(2,1)S(1)}, u32[]{:S(2)}, u32[]{:S(2)}) collective-permute-start(bf16[128,1024]{0,1:T(8,128)(2,1)} %bitcast), channel_id=1, source_target_pairs={{0,40},{8,48},{16,56},{24,64},{32,72},{40,80},{48,88},{56,96},{64,... | collective-permute-start | bytes 786440 | tf_op jit(solution)/shard_map/ppermute | solution.py:34
  102.3 2.8 collective-permute-start.4
  105.4 2.8 collective-permute-start.5
  108.3 2.8 collective-permute-start.6
  111.1 3.5 collective-permute-start.7
  122.6 1.8 copy.107
  129.6 6.1 fusion.53
  135.7 4.8 fusion.9
  140.5 3.7 fusion.57
  148.7 1.8 copy.146
  151.8 1.8 copy.145
  154.9 1.8 copy.144
  162.8 28.2 %collective-permute-done.39 = bf16[128,1024]{1,0:T(8,128)(2,1)} collective-permute-done((bf16[128,1024]{1,0:T(8,128)(2,1)}, bf16[128,1024]{1,0:T(8,128)(2,1)}, u32[]{:S(2)}, u32[]{:S(2)}) %collective-permute-start.39) | collective-permute-done | bytes 262176 | tf_op jit(solution)/shard_map/ppermute | solution.py:34
  196.2 10.7 %collective-permute-done.34 = bf16[128,1024]{1,0:T(8,128)(2,1)} collective-permute-done((bf16[128,1024]{1,0:T(8,128)(2,1)}, bf16[128,1024]{1,0:T(8,128)(2,1)}, u32[]{:S(2)}, u32[]{:S(2)}) %collective-permute-start.34) | collective-permute-done | bytes 262176 | tf_op jit(solution)/shard_map/ppermute | solution.py:34
  206.9 4.7 collective-permute-done.32
  211.7 1.9 add_convert_fusion
  213.6 4.4 stack.2
  218.0 30.3 %all-to-all-start = ((bf16[32,128,1024]{2,1,0:T(8,128)(2,1)}), bf16[32,128,1024]{2,1,0:T(8,128)(2,1)}, u32[]{:S(2)}, u32[]{:S(2)}) async-start(bf16[32,128,1024]{2,1,0:T(8,128)(2,1)} %stack.2), calls=%async_computation | async-start | bytes 16777216 | tf_op jit(solution)/shard_map/all_to_all | solution.py:24
  249.1 4.0 collective-permute-start.16
  253.1 5.2 collective-permute-start.17
  258.3 4.6 collective-permute-start.18
  262.9 3.2 collective-permute-start.19
  266.1 2.9 collective-permute-start.20
  269.1 168.1 %collective-permute-done.16 = bf16[128,1024]{0,1:T(8,128)(2,1)S(1)} collective-permute-done((bf16[128,1024]{0,1:T(8,128)(2,1)}, bf16[128,1024]{0,1:T(8,128)(2,1)S(1)}, u32[]{:S(2)}, u32[]{:S(2)}) %collective-permute-start.16) | collective-permute-done | bytes 262176 | tf_op jit(solution)/shard_map/ppermute | solution.py:34
  437.1 5.5 collective-permute-start.21
  442.9 13.4 %collective-permute-start.22 = (bf16[128,1024]{0,1:T(8,128)(2,1)}, bf16[128,1024]{0,1:T(8,128)(2,1)}, u32[]{:S(2)}, u32[]{:S(2)}) collective-permute-start(bf16[128,1024]{0,1:T(8,128)(2,1)} %bitcast.15), channel_id=1, source_target_pairs={{0,16},{8,24},{16,32},{24,40},{32,48},{40,56},{48,64},{56,72},{64,... | collective-permute-start | bytes 786440 | tf_op jit(solution)/shard_map/ppermute | solution.py:34
  456.4 8.9 %collective-permute-start.23 = (bf16[128,1024]{0,1:T(8,128)(2,1)}, bf16[128,1024]{0,1:T(8,128)(2,1)}, u32[]{:S(2)}, u32[]{:S(2)}) collective-permute-start(bf16[128,1024]{0,1:T(8,128)(2,1)} %bitcast.15), channel_id=1, source_target_pairs={{0,8},{8,16},{16,24},{24,32},{32,40},{40,48},{48,56},{56,64},{64,7... | collective-permute-start | bytes 786440 | tf_op jit(solution)/shard_map/ppermute | solution.py:34
  465.3 1.9 copy.120
  469.0 1.8 copy.113
  470.8 1.8 copy.114
  472.6 1.8 copy.115
  476.1 1.8 copy.117
  477.9 1.8 copy.118
  479.7 1.8 copy.119
  486.9 3.5 fusion.34
  493.2 3.7 fusion.56
  498.4 1.8 copy.137
  501.4 1.8 copy.136
  504.5 1.8 copy.135
  507.8 6.2 fusion.31
  513.9 18.2 %fusion = f32[24,1024]{1,0:T(8,128)S(1)} fusion(f32[168,1024]{1,0:T(8,128)} %fusion.31), kind=kCustom, calls=%all-reduce-scatter | all-reduce-scatter fusion | flops 196609 | bytes 787456
  532.8 2.3 collective-permute-start.40
  548.4 3.4 fusion.28
  555.8 5.8 collective-permute-done.28
  561.6 4.1 collective-permute-done.27
  565.7 9.3 %collective-permute-done.25 = bf16[128,1024]{1,0:T(8,128)(2,1)} collective-permute-done((bf16[128,1024]{1,0:T(8,128)(2,1)}, bf16[128,1024]{1,0:T(8,128)(2,1)}, u32[]{:S(2)}, u32[]{:S(2)}) %collective-permute-start.25) | collective-permute-done | bytes 262176 | tf_op jit(solution)/shard_map/ppermute | solution.py:34
  575.0 2.6 fusion.44
  577.6 103.5 %psum.7 = f32[]{:T(128)} all-reduce(f32[]{:T(128)} %multiply_reduce_fusion), channel_id=1, replica_groups=mesh['ctx'=32,'dp'=8] {'ctx','dp'}, use_global_device_ids=true, to_apply=%region_5.6 | all-reduce | flops 1 | bytes 8 | tf_op jit(solution)/shard_map/psum | solution.py:168
  682.5 13.5 %all-gather = bf16[8,21,1024]{2,1,0:T(8,128)(2,1)S(1)} all-gather(bf16[1,21,1024]{2,1,0:T(8,128)(2,1)S(1)} %get-tuple-element.28), channel_id=1, replica_groups=mesh['ctx'=32,'dp'=8] {'dp'}, dimensions={0}, use_global_device_ids=true | all-gather | bytes 387072 | tf_op jit(solution)/shard_map/all_gather | solution.py:175
  (180 shorter events, 72.9 us)
Async XLA Ops:
  1.3 34.0 %collective-permute-start.8 = (bf16[128]{0:T(256)(128)(2,1)S(1)}, bf16[128]{0:T(256)(128)(2,1)S(1)}, u32[]{:S(2)}, u32[]{:S(2)}) collective-permute-start(bf16[128]{0:T(256)(128)(2,1)S(1)} %convert_bitcast_fusion.1), channel_id=1, source_target_pairs={{0,64},{8,72},{16,80},{24,88},{32,96},{40,104},{48,112},{56,120},{... | collective-permute-start | bytes 776 | tf_op jit(solution)/shard_map/ppermute | solution.py:34
  7.0 34.0 %collective-permute-start.9 = (bf16[128]{0:T(256)(128)(2,1)S(1)}, bf16[128]{0:T(256)(128)(2,1)S(1)}, u32[]{:S(2)}, u32[]{:S(2)}) collective-permute-start(bf16[128]{0:T(256)(128)(2,1)S(1)} %convert_bitcast_fusion.1), channel_id=1, source_target_pairs={{0,56},{8,64},{16,72},{24,80},{32,88},{40,96},{48,104},{56,112},{6... | collective-permute-start | bytes 776 | tf_op jit(solution)/shard_map/ppermute | solution.py:34
  14.5 18.2 %copy-start.14 = (bf16[1,128,2048]{2,1,0:T(8,128)(2,1)S(1)}, bf16[1,128,2048]{2,1,0:T(8,128)(2,1)}, u32[]{:S(2)}) copy-start(bf16[1,128,2048]{2,1,0:T(8,128)(2,1)} %param.13) | copy-start | bytes 1572868
  14.5 90.9 %collective-permute-start = (bf16[128,1024]{0,1:T(8,128)(2,1)}, bf16[128,1024]{0,1:T(8,128)(2,1)S(1)}, u32[]{:S(2)}, u32[]{:S(2)}) collective-permute-start(bf16[128,1024]{0,1:T(8,128)(2,1)} %bitcast), channel_id=1, source_target_pairs={{0,64},{8,72},{16,80},{24,88},{32,96},{40,104},{48,112},{56,120},{... | collective-permute-start | bytes 786440 | tf_op jit(solution)/shard_map/ppermute | solution.py:34
  19.9 88.3 %collective-permute-start.1 = (bf16[128,1024]{0,1:T(8,128)(2,1)}, bf16[128,1024]{0,1:T(8,128)(2,1)S(1)}, u32[]{:S(2)}, u32[]{:S(2)}) collective-permute-start(bf16[128,1024]{0,1:T(8,128)(2,1)} %bitcast), channel_id=1, source_target_pairs={{0,56},{8,64},{16,72},{24,80},{32,88},{40,96},{48,104},{56,112},{6... | collective-permute-start | bytes 786440 | tf_op jit(solution)/shard_map/ppermute | solution.py:34
  23.3 87.8 %collective-permute-start.2 = (bf16[128,1024]{0,1:T(8,128)(2,1)}, bf16[128,1024]{0,1:T(8,128)(2,1)S(1)}, u32[]{:S(2)}, u32[]{:S(2)}) collective-permute-start(bf16[128,1024]{0,1:T(8,128)(2,1)} %bitcast), channel_id=1, source_target_pairs={{0,48},{8,56},{16,64},{24,72},{32,80},{40,88},{48,96},{56,104},{64... | collective-permute-start | bytes 786440 | tf_op jit(solution)/shard_map/ppermute | solution.py:34
  27.7 5.3 copy-start.15
  27.7 77.7 %copy-start.25 = (s32[1,128]{1,0:T(1,128)S(1)}, s32[1,128]{1,0:T(1,128)}, u32[]{:S(2)}) copy-start(s32[1,128]{1,0:T(1,128)} %param.14) | copy-start | bytes 1540
  27.7 185.8 %all-to-all-start.1 = ((bf16[128,32,168]{0,2,1:T(8,128)(2,1)}), bf16[128,32,168]{0,2,1:T(8,128)(2,1)}, u32[]{:S(2)}, u32[]{:S(2)}) async-start(bf16[128,32,168]{0,2,1:T(8,128)(2,1)} %bitcast.61), calls=%async_computation.1 | async-start | bytes 2752512 | tf_op jit(solution)/shard_map/all_to_all | solution.py:160
  33.0 107.5 %copy-start.2 = (bf16[1,128,2048]{1,2,0:T(8,128)(2,1)}, bf16[1,128,2048]{1,2,0:T(8,128)(2,1)S(1)}, u32[]{:S(2)}) copy-start(bf16[1,128,2048]{1,2,0:T(8,128)(2,1)S(1)} %copy.121) | copy-start | bytes 1572868
  33.3 96.3 %copy-start.4 = (bf16[1,128,2048]{1,2,0:T(8,128)(2,1)}, bf16[1,128,2048]{1,2,0:T(8,128)(2,1)S(1)}, u32[]{:S(2)}) copy-start(bf16[1,128,2048]{1,2,0:T(8,128)(2,1)S(1)} %copy.165) | copy-start | bytes 1572868
  35.3 30.3 %collective-permute-start.10 = (bf16[128]{0:T(256)(128)(2,1)S(1)}, bf16[128]{0:T(256)(128)(2,1)S(1)}, u32[]{:S(2)}, u32[]{:S(2)}) collective-permute-start(bf16[128]{0:T(256)(128)(2,1)S(1)} %convert_bitcast_fusion.1), channel_id=1, source_target_pairs={{0,48},{8,56},{16,64},{24,72},{32,80},{40,88},{48,96},{56,104},{64... | collective-permute-start | bytes 776 | tf_op jit(solution)/shard_map/ppermute | solution.py:34
  41.0 34.7 %collective-permute-start.11 = (bf16[128]{0:T(256)(128)(2,1)S(1)}, bf16[128]{0:T(256)(128)(2,1)S(1)}, u32[]{:S(2)}, u32[]{:S(2)}) collective-permute-start(bf16[128]{0:T(256)(128)(2,1)S(1)} %convert_bitcast_fusion.1), channel_id=1, source_target_pairs={{0,40},{8,48},{16,56},{24,64},{32,72},{40,80},{48,88},{56,96},{64,... | collective-permute-start | bytes 776 | tf_op jit(solution)/shard_map/ppermute | solution.py:34
  65.6 24.2 %collective-permute-start.12 = (bf16[128]{0:T(256)(128)(2,1)S(1)}, bf16[128]{0:T(256)(128)(2,1)S(1)}, u32[]{:S(2)}, u32[]{:S(2)}) collective-permute-start(bf16[128]{0:T(256)(128)(2,1)S(1)} %convert_bitcast_fusion.1), channel_id=1, source_target_pairs={{0,32},{8,40},{16,48},{24,56},{32,64},{40,72},{48,80},{56,88},{64,... | collective-permute-start | bytes 776 | tf_op jit(solution)/shard_map/ppermute | solution.py:34
  75.7 15.7 %collective-permute-start.13 = (bf16[128]{0:T(256)(128)(2,1)S(1)}, bf16[128]{0:T(256)(128)(2,1)S(1)}, u32[]{:S(2)}, u32[]{:S(2)}) collective-permute-start(bf16[128]{0:T(256)(128)(2,1)S(1)} %convert_bitcast_fusion.1), channel_id=1, source_target_pairs={{0,24},{8,32},{16,40},{24,48},{32,56},{40,64},{48,72},{56,80},{64,... | collective-permute-start | bytes 776 | tf_op jit(solution)/shard_map/ppermute | solution.py:34
  89.8 4.9 collective-permute-start.14
  91.4 10.9 %collective-permute-start.15 = (bf16[128]{0:T(256)(128)(2,1)S(1)}, bf16[128]{0:T(256)(128)(2,1)S(1)}, u32[]{:S(2)}, u32[]{:S(2)}) collective-permute-start(bf16[128]{0:T(256)(128)(2,1)S(1)} %convert_bitcast_fusion.1), channel_id=1, source_target_pairs={{0,8},{8,16},{16,24},{24,32},{32,40},{40,48},{48,56},{56,64},{64,7... | collective-permute-start | bytes 776 | tf_op jit(solution)/shard_map/ppermute | solution.py:34
  94.7 23.4 %collective-permute-start.3 = (bf16[128,1024]{0,1:T(8,128)(2,1)}, bf16[128,1024]{0,1:T(8,128)(2,1)S(1)}, u32[]{:S(2)}, u32[]{:S(2)}) collective-permute-start(bf16[128,1024]{0,1:T(8,128)(2,1)} %bitcast), channel_id=1, source_target_pairs={{0,40},{8,48},{16,56},{24,64},{32,72},{40,80},{48,88},{56,96},{64,... | collective-permute-start | bytes 786440 | tf_op jit(solution)/shard_map/ppermute | solution.py:34
  102.3 16.7 %collective-permute-start.4 = (bf16[128,1024]{0,1:T(8,128)(2,1)}, bf16[128,1024]{0,1:T(8,128)(2,1)S(1)}, u32[]{:S(2)}, u32[]{:S(2)}) collective-permute-start(bf16[128,1024]{0,1:T(8,128)(2,1)} %bitcast), channel_id=1, source_target_pairs={{0,32},{8,40},{16,48},{24,56},{32,64},{40,72},{48,80},{56,88},{64,... | collective-permute-start | bytes 786440 | tf_op jit(solution)/shard_map/ppermute | solution.py:34
  105.4 14.5 %collective-permute-start.5 = (bf16[128,1024]{0,1:T(8,128)(2,1)}, bf16[128,1024]{0,1:T(8,128)(2,1)S(1)}, u32[]{:S(2)}, u32[]{:S(2)}) collective-permute-start(bf16[128,1024]{0,1:T(8,128)(2,1)} %bitcast), channel_id=1, source_target_pairs={{0,24},{8,32},{16,40},{24,48},{32,56},{40,64},{48,72},{56,80},{64,... | collective-permute-start | bytes 786440 | tf_op jit(solution)/shard_map/ppermute | solution.py:34
  108.3 12.5 %collective-permute-start.6 = (bf16[128,1024]{0,1:T(8,128)(2,1)}, bf16[128,1024]{0,1:T(8,128)(2,1)S(1)}, u32[]{:S(2)}, u32[]{:S(2)}) collective-permute-start(bf16[128,1024]{0,1:T(8,128)(2,1)} %bitcast), channel_id=1, source_target_pairs={{0,16},{8,24},{16,32},{24,40},{32,48},{40,56},{48,64},{56,72},{64,... | collective-permute-start | bytes 786440 | tf_op jit(solution)/shard_map/ppermute | solution.py:34
  111.1 11.5 %collective-permute-start.7 = (bf16[128,1024]{0,1:T(8,128)(2,1)}, bf16[128,1024]{0,1:T(8,128)(2,1)}, u32[]{:S(2)}, u32[]{:S(2)}) collective-permute-start(bf16[128,1024]{0,1:T(8,128)(2,1)} %bitcast), channel_id=1, source_target_pairs={{0,8},{8,16},{16,24},{24,32},{32,40},{40,48},{48,56},{56,64},{64,7... | collective-permute-start | bytes 786440 | tf_op jit(solution)/shard_map/ppermute | solution.py:34
  124.4 5.1 copy-start.12
  124.4 5.1 copy-start.6
  147.4 43.6 %collective-permute-start.39 = (bf16[128,1024]{1,0:T(8,128)(2,1)}, bf16[128,1024]{1,0:T(8,128)(2,1)}, u32[]{:S(2)}, u32[]{:S(2)}) collective-permute-start(bf16[128,1024]{1,0:T(8,128)(2,1)} %copy.147), channel_id=1, source_target_pairs={{64,0},{72,8},{80,16},{88,24},{96,32},{104,40},{112,48},{120,56},{... | collective-permute-start | bytes 786440 | tf_op jit(solution)/shard_map/ppermute | solution.py:34
  150.5 41.8 %collective-permute-start.38 = (bf16[128,1024]{1,0:T(8,128)(2,1)}, bf16[128,1024]{1,0:T(8,128)(2,1)}, u32[]{:S(2)}, u32[]{:S(2)}) collective-permute-start(bf16[128,1024]{1,0:T(8,128)(2,1)} %copy.146), channel_id=1, source_target_pairs={{56,0},{64,8},{72,16},{80,24},{88,32},{96,40},{104,48},{112,56},{1... | collective-permute-start | bytes 786440 | tf_op jit(solution)/shard_map/ppermute | solution.py:34
  153.6 40.0 %collective-permute-start.37 = (bf16[128,1024]{1,0:T(8,128)(2,1)}, bf16[128,1024]{1,0:T(8,128)(2,1)}, u32[]{:S(2)}, u32[]{:S(2)}) collective-permute-start(bf16[128,1024]{1,0:T(8,128)(2,1)} %copy.145), channel_id=1, source_target_pairs={{48,0},{56,8},{64,16},{72,24},{80,32},{88,40},{96,48},{104,56},{11... | collective-permute-start | bytes 786440 | tf_op jit(solution)/shard_map/ppermute | solution.py:34
  156.7 39.5 %collective-permute-start.36 = (bf16[128,1024]{1,0:T(8,128)(2,1)}, bf16[128,1024]{1,0:T(8,128)(2,1)}, u32[]{:S(2)}, u32[]{:S(2)}) collective-permute-start(bf16[128,1024]{1,0:T(8,128)(2,1)} %copy.144), channel_id=1, source_target_pairs={{40,0},{48,8},{56,16},{64,24},{72,32},{80,40},{88,48},{96,56},{104... | collective-permute-start | bytes 786440 | tf_op jit(solution)/shard_map/ppermute | solution.py:34
  158.8 37.4 %collective-permute-start.35 = (bf16[128,1024]{1,0:T(8,128)(2,1)}, bf16[128,1024]{1,0:T(8,128)(2,1)}, u32[]{:S(2)}, u32[]{:S(2)}) collective-permute-start(bf16[128,1024]{1,0:T(8,128)(2,1)} %copy.143), channel_id=1, source_target_pairs={{32,0},{40,8},{48,16},{56,24},{64,32},{72,40},{80,48},{88,56},{96,... | collective-permute-start | bytes 786440 | tf_op jit(solution)/shard_map/ppermute | solution.py:34
  191.0 15.9 %collective-permute-start.34 = (bf16[128,1024]{1,0:T(8,128)(2,1)}, bf16[128,1024]{1,0:T(8,128)(2,1)}, u32[]{:S(2)}, u32[]{:S(2)}) collective-permute-start(bf16[128,1024]{1,0:T(8,128)(2,1)} %copy.142), channel_id=1, source_target_pairs={{24,0},{32,8},{40,16},{48,24},{56,32},{64,40},{72,48},{80,56},{88,... | collective-permute-start | bytes 786440 | tf_op jit(solution)/shard_map/ppermute | solution.py:34
  192.3 14.6 %collective-permute-start.33 = (bf16[128,1024]{1,0:T(8,128)(2,1)}, bf16[128,1024]{1,0:T(8,128)(2,1)}, u32[]{:S(2)}, u32[]{:S(2)}) collective-permute-start(bf16[128,1024]{1,0:T(8,128)(2,1)} %copy.141), channel_id=1, source_target_pairs={{16,0},{24,8},{32,16},{40,24},{48,32},{56,40},{64,48},{72,56},{80,... | collective-permute-start | bytes 786440 | tf_op jit(solution)/shard_map/ppermute | solution.py:34
  193.6 18.1 %collective-permute-start.32 = (bf16[128,1024]{1,0:T(8,128)(2,1)}, bf16[128,1024]{1,0:T(8,128)(2,1)}, u32[]{:S(2)}, u32[]{:S(2)}) collective-permute-start(bf16[128,1024]{1,0:T(8,128)(2,1)} %copy.139), channel_id=1, source_target_pairs={{8,0},{16,8},{24,16},{32,24},{40,32},{48,40},{56,48},{64,56},{72,6... | collective-permute-start | bytes 786440 | tf_op jit(solution)/shard_map/ppermute | solution.py:34
  218.0 30.3 %copy-start.16 = (bf16[1,128,1024]{2,1,0:T(8,128)(2,1)S(1)}, bf16[1,128,1024]{2,1,0:T(8,128)(2,1)}, u32[]{:S(2)}) copy-start(bf16[1,128,1024]{2,1,0:T(8,128)(2,1)} %param.12) | copy-start | bytes 786436
  218.0 289.8 %all-to-all-start = ((bf16[32,128,1024]{2,1,0:T(8,128)(2,1)}), bf16[32,128,1024]{2,1,0:T(8,128)(2,1)}, u32[]{:S(2)}, u32[]{:S(2)}) async-start(bf16[32,128,1024]{2,1,0:T(8,128)(2,1)} %stack.2), calls=%async_computation | async-start | bytes 16777216 | tf_op jit(solution)/shard_map/all_to_all | solution.py:24
  249.1 188.0 %collective-permute-start.16 = (bf16[128,1024]{0,1:T(8,128)(2,1)}, bf16[128,1024]{0,1:T(8,128)(2,1)S(1)}, u32[]{:S(2)}, u32[]{:S(2)}) collective-permute-start(bf16[128,1024]{0,1:T(8,128)(2,1)} %bitcast.15), channel_id=1, source_target_pairs={{0,64},{8,72},{16,80},{24,88},{32,96},{40,104},{48,112},{56,120},{... | collective-permute-start | bytes 786440 | tf_op jit(solution)/shard_map/ppermute | solution.py:34
  253.1 189.8 %collective-permute-start.17 = (bf16[128,1024]{0,1:T(8,128)(2,1)}, bf16[128,1024]{0,1:T(8,128)(2,1)S(1)}, u32[]{:S(2)}, u32[]{:S(2)}) collective-permute-start(bf16[128,1024]{0,1:T(8,128)(2,1)} %bitcast.15), channel_id=1, source_target_pairs={{0,56},{8,64},{16,72},{24,80},{32,88},{40,96},{48,104},{56,112},{6... | collective-permute-start | bytes 786440 | tf_op jit(solution)/shard_map/ppermute | solution.py:34
  258.3 198.1 %collective-permute-start.18 = (bf16[128,1024]{0,1:T(8,128)(2,1)}, bf16[128,1024]{0,1:T(8,128)(2,1)S(1)}, u32[]{:S(2)}, u32[]{:S(2)}) collective-permute-start(bf16[128,1024]{0,1:T(8,128)(2,1)} %bitcast.15), channel_id=1, source_target_pairs={{0,48},{8,56},{16,64},{24,72},{32,80},{40,88},{48,96},{56,104},{64... | collective-permute-start | bytes 786440 | tf_op jit(solution)/shard_map/ppermute | solution.py:34
  262.9 209.6 %collective-permute-start.19 = (bf16[128,1024]{0,1:T(8,128)(2,1)}, bf16[128,1024]{0,1:T(8,128)(2,1)}, u32[]{:S(2)}, u32[]{:S(2)}) collective-permute-start(bf16[128,1024]{0,1:T(8,128)(2,1)} %bitcast.15), channel_id=1, source_target_pairs={{0,40},{8,48},{16,56},{24,64},{32,72},{40,80},{48,88},{56,96},{64,... | collective-permute-start | bytes 786440 | tf_op jit(solution)/shard_map/ppermute | solution.py:34
  266.1 208.2 %collective-permute-start.20 = (bf16[128,1024]{0,1:T(8,128)(2,1)}, bf16[128,1024]{0,1:T(8,128)(2,1)}, u32[]{:S(2)}, u32[]{:S(2)}) collective-permute-start(bf16[128,1024]{0,1:T(8,128)(2,1)} %bitcast.15), channel_id=1, source_target_pairs={{0,32},{8,40},{16,48},{24,56},{32,64},{40,72},{48,80},{56,88},{64,... | collective-permute-start | bytes 786440 | tf_op jit(solution)/shard_map/ppermute | solution.py:34
  437.1 28.2 %copy-start.17 = (bf16[128,1024]{0,1:T(8,128)(2,1)}, bf16[128,1024]{0,1:T(8,128)(2,1)S(1)}, u32[]{:S(2)}) copy-start(bf16[128,1024]{0,1:T(8,128)(2,1)S(1)} %collective-permute-done.16) | copy-start | bytes 786436
  437.1 39.0 %collective-permute-start.21 = (bf16[128,1024]{0,1:T(8,128)(2,1)}, bf16[128,1024]{0,1:T(8,128)(2,1)}, u32[]{:S(2)}, u32[]{:S(2)}) collective-permute-start(bf16[128,1024]{0,1:T(8,128)(2,1)} %bitcast.15), channel_id=1, source_target_pairs={{0,24},{8,32},{16,40},{24,48},{32,56},{40,64},{48,72},{56,80},{64,... | collective-permute-start | bytes 786440 | tf_op jit(solution)/shard_map/ppermute | solution.py:34
  442.9 22.4 %copy-start.18 = (bf16[128,1024]{0,1:T(8,128)(2,1)}, bf16[128,1024]{0,1:T(8,128)(2,1)S(1)}, u32[]{:S(2)}) copy-start(bf16[128,1024]{0,1:T(8,128)(2,1)S(1)} %collective-permute-done.17) | copy-start | bytes 786436
  442.9 35.0 %collective-permute-start.22 = (bf16[128,1024]{0,1:T(8,128)(2,1)}, bf16[128,1024]{0,1:T(8,128)(2,1)}, u32[]{:S(2)}, u32[]{:S(2)}) collective-permute-start(bf16[128,1024]{0,1:T(8,128)(2,1)} %bitcast.15), channel_id=1, source_target_pairs={{0,16},{8,24},{16,32},{24,40},{32,48},{40,56},{48,64},{56,72},{64,... | collective-permute-start | bytes 786440 | tf_op jit(solution)/shard_map/ppermute | solution.py:34
  456.4 8.9 %copy-start.19 = (bf16[128,1024]{0,1:T(8,128)(2,1)}, bf16[128,1024]{0,1:T(8,128)(2,1)S(1)}, u32[]{:S(2)}) copy-start(bf16[128,1024]{0,1:T(8,128)(2,1)S(1)} %collective-permute-done.18) | copy-start | bytes 786436
  456.4 23.3 %collective-permute-start.23 = (bf16[128,1024]{0,1:T(8,128)(2,1)}, bf16[128,1024]{0,1:T(8,128)(2,1)}, u32[]{:S(2)}, u32[]{:S(2)}) collective-permute-start(bf16[128,1024]{0,1:T(8,128)(2,1)} %bitcast.15), channel_id=1, source_target_pairs={{0,8},{8,16},{16,24},{24,32},{32,40},{40,48},{48,56},{56,64},{64,7... | collective-permute-start | bytes 786440 | tf_op jit(solution)/shard_map/ppermute | solution.py:34
  465.3 25.1 %slice-start = ((s8[9437184]{0:T(1024)(128)(4,1)}), s8[1048576]{0:T(1024)(128)(4,1)S(1)}, s32[]{:S(2)}) async-start(s8[9437184]{0:T(1024)(128)(4,1)} %bitcast.144), calls=%async_computation.2 | async-start | bytes 2097152
  481.5 5.1 copy-start.8
  481.5 5.1 copy-start.10
  481.5 5.2 copy-start.11
  481.5 5.2 copy-start.7
  481.5 5.3 copy-start.3
  500.2 42.8 %collective-permute-start.31 = (bf16[128,1024]{1,0:T(8,128)(2,1)}, bf16[128,1024]{1,0:T(8,128)(2,1)}, u32[]{:S(2)}, u32[]{:S(2)}) collective-permute-start(bf16[128,1024]{1,0:T(8,128)(2,1)} %copy.137), channel_id=1, source_target_pairs={{64,0},{72,8},{80,16},{88,24},{96,32},{104,40},{112,48},{120,56},{... | collective-permute-start | bytes 786440 | tf_op jit(solution)/shard_map/ppermute | solution.py:34
  503.2 41.0 %collective-permute-start.30 = (bf16[128,1024]{1,0:T(8,128)(2,1)}, bf16[128,1024]{1,0:T(8,128)(2,1)}, u32[]{:S(2)}, u32[]{:S(2)}) collective-permute-start(bf16[128,1024]{1,0:T(8,128)(2,1)} %copy.136), channel_id=1, source_target_pairs={{56,0},{64,8},{72,16},{80,24},{88,32},{96,40},{104,48},{112,56},{1... | collective-permute-start | bytes 786440 | tf_op jit(solution)/shard_map/ppermute | solution.py:34
  506.3 28.9 %copy-start.24 = (u32[256]{0:T(256)S(1)}, u32[256]{0:T(256)}, u32[]{:S(2)}) copy-start(u32[256]{0:T(256)} %constant.59) | copy-start | bytes 3076
  506.3 39.4 %collective-permute-start.29 = (bf16[128,1024]{1,0:T(8,128)(2,1)}, bf16[128,1024]{1,0:T(8,128)(2,1)}, u32[]{:S(2)}, u32[]{:S(2)}) collective-permute-start(bf16[128,1024]{1,0:T(8,128)(2,1)} %copy.135), channel_id=1, source_target_pairs={{48,0},{56,8},{64,16},{72,24},{80,32},{88,40},{96,48},{104,56},{11... | collective-permute-start | bytes 786440 | tf_op jit(solution)/shard_map/ppermute | solution.py:34
  532.8 14.2 %collective-permute-start.40 = (f32[21,1024]{1,0:T(8,128)}, f32[21,1024]{1,0:T(8,128)}, u32[]{:S(2)}, u32[]{:S(2)}) collective-permute-start(f32[21,1024]{1,0:T(8,128)} %slice.130), channel_id=1, source_target_pairs={{0,1},{1,2},{2,3},{3,4},{4,5},{5,6},{6,7},{8,9},{9,10},{10,11},{11... | collective-permute-start | bytes 258056
  538.2 23.4 %collective-permute-start.28 = (bf16[128,1024]{1,0:T(8,128)(2,1)}, bf16[128,1024]{1,0:T(8,128)(2,1)}, u32[]{:S(2)}, u32[]{:S(2)}) collective-permute-start(bf16[128,1024]{1,0:T(8,128)(2,1)} %copy.134), channel_id=1, source_target_pairs={{40,0},{48,8},{56,16},{64,24},{72,32},{80,40},{88,48},{96,56},{104... | collective-permute-start | bytes 786440 | tf_op jit(solution)/shard_map/ppermute | solution.py:34
  542.9 22.7 %collective-permute-start.27 = (bf16[128,1024]{1,0:T(8,128)(2,1)}, bf16[128,1024]{1,0:T(8,128)(2,1)}, u32[]{:S(2)}, u32[]{:S(2)}) collective-permute-start(bf16[128,1024]{1,0:T(8,128)(2,1)} %copy.133), channel_id=1, source_target_pairs={{32,0},{40,8},{48,16},{56,24},{64,32},{72,40},{80,48},{88,56},{96,... | collective-permute-start | bytes 786440 | tf_op jit(solution)/shard_map/ppermute | solution.py:34
  544.2 21.4 %collective-permute-start.26 = (bf16[128,1024]{1,0:T(8,128)(2,1)}, bf16[128,1024]{1,0:T(8,128)(2,1)}, u32[]{:S(2)}, u32[]{:S(2)}) collective-permute-start(bf16[128,1024]{1,0:T(8,128)(2,1)} %copy.132), channel_id=1, source_target_pairs={{24,0},{32,8},{40,16},{48,24},{56,32},{64,40},{72,48},{80,56},{88,... | collective-permute-start | bytes 786440 | tf_op jit(solution)/shard_map/ppermute | solution.py:34
  545.8 29.2 %collective-permute-start.25 = (bf16[128,1024]{1,0:T(8,128)(2,1)}, bf16[128,1024]{1,0:T(8,128)(2,1)}, u32[]{:S(2)}, u32[]{:S(2)}) collective-permute-start(bf16[128,1024]{1,0:T(8,128)(2,1)} %copy.131), channel_id=1, source_target_pairs={{16,0},{24,8},{32,16},{40,24},{48,32},{56,40},{64,48},{72,56},{80,... | collective-permute-start | bytes 786440 | tf_op jit(solution)/shard_map/ppermute | solution.py:34
  547.1 27.9 %collective-permute-start.24 = (bf16[128,1024]{1,0:T(8,128)(2,1)}, bf16[128,1024]{1,0:T(8,128)(2,1)}, u32[]{:S(2)}, u32[]{:S(2)}) collective-permute-start(bf16[128,1024]{1,0:T(8,128)(2,1)} %copy.129), channel_id=1, source_target_pairs={{8,0},{16,8},{24,16},{32,24},{40,32},{48,40},{56,48},{64,56},{72,6... | collective-permute-start | bytes 786440 | tf_op jit(solution)/shard_map/ppermute | solution.py:34
  553.8 127.9 %copy-start.20 = (f32[21,1024]{1,0:T(8,128)S(1)}, f32[21,1024]{1,0:T(8,128)}, u32[]{:S(2)}) copy-start(f32[21,1024]{1,0:T(8,128)} %param.15) | copy-start | bytes 258052
  553.8 127.9 %copy-start.21 = (f32[21,1024]{1,0:T(8,128)S(1)}, f32[21,1024]{1,0:T(8,128)}, u32[]{:S(2)}) copy-start(f32[21,1024]{1,0:T(8,128)} %param.16) | copy-start | bytes 258052
  553.8 127.9 %copy-start.22 = (f32[21,1024]{1,0:T(8,128)S(1)}, f32[21,1024]{1,0:T(8,128)}, u32[]{:S(2)}) copy-start(f32[21,1024]{1,0:T(8,128)} %param.17) | copy-start | bytes 258052
  (8 other events, 31.9 us)
